TPU v7x, 256 devices: a whole 4x4x8 slice. The times are simulated.
256 devices in a mesh: dp: 64 (over y, z, core), mp: 4 (over x).
Axes of the slice: x: 4, y: 4, z: 8, core: 2. Of those that a mesh axis runs over, the one named last changes fastest.
Arguments:
- queries: bfloat16 [32768, 1024], P('dp', 'mp'), may hold values from -20 to 20
- passages: bfloat16 [262144, 1024], P('dp', 'mp'), may hold values from -6 to 6
- positives: int32 [32768], P('dp'), may hold values from 0 to 4095, as said below
- negatives: int32 [64, 64], replicated, may hold values from -1 to 31, as said below
Outputs:
- losses: float32 [32768], P('dp')
- query_grad: float32 [32768, 1024], P('dp', 'mp')
- passage_grad: float32 [262144, 1024], P('dp', 'mp')
Inputs may be any that keep to these rules, and one draw needn't show every extreme that they name: Within each dp index the 512 positives of its query block are distinct. `negatives`: each row names between 16 and 64 blocks (entries >= 0); some row names 64.
All inputs are finite; a program needn't handle non-finite values.
Results may differ from a plain program's by a relative error of at most 0.0075.
Values may be sent and summed in bfloat16 or wider, within the bound.
No kernel may reach another device: no remote copies, remote signals or barrier semaphores. Data moves between devices by JAX's collectives and lax.ppermute only.
A program may use at most 128 MiB of HBM per device.

v0:
```python
import jax
import jax.numpy as jnp
from jax import lax
from jax.sharding import PartitionSpec as P

PBS = 128
HALVES = 2


def body(queries, passages, positives, negatives):
    dp_count = lax.axis_size("dp")
    mp_count = lax.axis_size("mp")
    own_index = lax.axis_index("dp")
    width_index = lax.axis_index("mp")
    query_rows, shard_width = queries.shape
    factor = (shard_width * mp_count) ** (-0.5)
    block_count = passages.shape[0] // PBS
    slots_per = dp_count // mp_count
    pos_per = query_rows // mp_count
    part = PBS // HALVES
    blocks = passages.reshape(block_count, PBS, shard_width)
    asked = lax.dynamic_index_in_dim(negatives, own_index, 1, keepdims=False)
    outgoing = jnp.take(blocks, jnp.maximum(asked, 0), axis=0)
    outgoing = jnp.where((asked >= 0)[:, None, None], outgoing, jnp.zeros_like(outgoing))
    wanted = lax.dynamic_index_in_dim(negatives, own_index, 0, keepdims=False)
    my_slots = lax.dynamic_slice_in_dim(wanted, width_index * slots_per, slots_per) >= 0
    q_full = lax.all_gather(queries, "mp", axis=1, tiled=True)
    q4 = q_full.reshape(query_rows, mp_count, shard_width)
    positive_rows = jnp.take(passages, positives, axis=0)
    mine, valid = ([], [])
    for h in range(HALVES):
        fetched = lax.all_to_all(
            outgoing[:, h * part : (h + 1) * part], "dp", split_axis=0, concat_axis=0, tiled=True
        )
        send = fetched.reshape(mp_count, slots_per * part, shard_width)
        ok = jnp.broadcast_to(my_slots[:, None], (slots_per, part)).reshape(-1)
        if h == 0:
            send = jnp.concatenate(
                [positive_rows.reshape(mp_count, pos_per, shard_width), send], axis=1
            )
            ok = jnp.concatenate([jnp.ones((pos_per,), bool), ok])
        mine.append(lax.all_to_all(send, "mp", split_axis=0, concat_axis=0, tiled=True))
        valid.append(ok)
    scores = [
        factor
        * lax.dot_general(c, q4, (((0, 2), (1, 2)), ((), ())), preferred_element_type=jnp.float32)
        for c in mine
    ]
    masked = [jnp.where(v[:, None], s, jnp.float32(-1e30)) for s, v in zip(scores, valid)]
    local_top = jnp.max(jnp.stack([jnp.max(x, axis=0) for x in masked]), axis=0)
    local_total = sum(
        (
            jnp.sum(jnp.where(v[:, None], jnp.exp(x - local_top), jnp.float32(0.0)), axis=0)
            for x, v in zip(masked, valid)
        )
    )
    target = (width_index * pos_per + jnp.arange(pos_per, dtype=jnp.int32))[:, None] == jnp.arange(
        query_rows, dtype=jnp.int32
    )[None, :]
    local_own = jnp.sum(jnp.where(target, scores[0][:pos_per], jnp.float32(0.0)), axis=0)
    stats = lax.all_gather(jnp.stack([local_top, local_total, local_own]), "mp", axis=0)
    top = jnp.max(stats[:, 0], axis=0)
    total = jnp.sum(stats[:, 1] * jnp.exp(stats[:, 0] - top), axis=0)
    own_score = jnp.sum(stats[:, 2], axis=0)
    lse = top + jnp.log(total)
    losses = lse - own_score
    grads = []
    for h in range(HALVES):
        prob = jnp.where(valid[h][:, None], jnp.exp(masked[h] - lse), jnp.float32(0.0))
        if h == 0:
            prob = jnp.concatenate([prob[:pos_per] - target.astype(jnp.float32), prob[pos_per:]])
        grads.append(prob.astype(jnp.bfloat16))
    query_part = sum(
        (
            lax.dot_general(g, c, (((0,), (1,)), ((), ())), preferred_element_type=jnp.float32)
            for g, c in zip(grads, mine)
        )
    )
    query_grad = lax.psum_scatter(factor * query_part, "mp", scatter_dimension=1, tiled=True)
    query_grad = query_grad.reshape(query_rows, shard_width)
    returned, pos_back = ([], None)
    for h in range(HALVES):
        cand = factor * jnp.dot(grads[h], q_full, preferred_element_type=jnp.float32)
        rows = cand.shape[0]
        pieces = []
        if h == 0:
            pos = cand[:pos_per]
            rounded = lax.reduce_precision(pos, exponent_bits=8, mantissa_bits=7)
            high = rounded.astype(jnp.bfloat16)
            low = (pos - rounded).astype(jnp.bfloat16)
            for x in (high, low):
                pieces.append(x.reshape(pos_per, mp_count, shard_width).transpose(1, 0, 2))
            cand = cand[pos_per:]
            rows -= pos_per
        neg = cand.astype(jnp.bfloat16).reshape(rows, mp_count, shard_width).transpose(1, 0, 2)
        pieces.append(neg)
        sent = lax.all_to_all(
            jnp.concatenate(pieces, axis=1), "mp", split_axis=0, concat_axis=0, tiled=True
        )
        if h == 0:
            pos_back = (
                sent[:, :pos_per].astype(jnp.float32)
                + sent[:, pos_per : 2 * pos_per].astype(jnp.float32)
            ).reshape(query_rows, shard_width)
            sent = sent[:, 2 * pos_per :]
        back = lax.all_to_all(
            sent.reshape(dp_count, part, shard_width), "dp", split_axis=0, concat_axis=0, tiled=True
        )
        returned.append(back)
    returned = jnp.concatenate(returned, axis=1).astype(jnp.float32)
    selector = (asked[None, :] == jnp.arange(block_count, dtype=jnp.int32)[:, None]).astype(
        jnp.float32
    )
    block_grad = jnp.einsum("kr,rpd->kpd", selector, returned, precision=lax.Precision.HIGHEST)
    passage_grad = block_grad.reshape(block_count * PBS, shard_width).at[positives].add(pos_back)
    return (losses, query_grad, passage_grad)


def solution(mesh):
    in_specs = (P("dp", "mp"), P("dp", "mp"), P("dp"), P())
    out_specs = (P("dp"), P("dp", "mp"), P("dp", "mp"))
    return jax.shard_map(body, mesh=mesh, in_specs=in_specs, out_specs=out_specs, check_vma=False)
```

profile of v0, /device:TPU:1, one launch (start us, length us, event | category | flops | bytes accessed | tf_op | source)
XLA Modules:
  0.0 430.8 jit_solution(1757947262718900918)
XLA Ops:
  9.3 2.8 gather_fusion.1
  12.1 2.7 select_select_fusion
  15.3 64.3 %all_to_all.40 = bf16[64,64,256]{2,1,0:T(8,128)(2,1)} all-to-all(bf16[64,64,256]{2,1,0:T(8,128)(2,1)S(1)} %get-tuple-element.12), channel_id=1, replica_groups=mesh['dp'=64,'mp'=4] {'dp'}, dimensions={0} | all-to-all | bytes 4194304 | tf_op jit(solution)/shard_map/all_to_all | solution.py:32
  79.7 57.0 %all_to_all.41 = bf16[64,64,256]{2,1,0:T(8,128)(2,1)} all-to-all(bf16[64,64,256]{2,1,0:T(8,128)(2,1)S(1)} %get-tuple-element.11), channel_id=1, replica_groups=mesh['dp'=64,'mp'=4] {'dp'}, dimensions={0} | all-to-all | bytes 4194304 | tf_op jit(solution)/shard_map/all_to_all | solution.py:32
  136.6 4.6 %all-to-all-start.3 = ((bf16[4,1024,256]{2,1,0:T(8,128)(2,1)}), bf16[4,1024,256]{2,1,0:T(8,128)(2,1)}, u32[]{:S(2)}, u32[]{:S(2)}) async-start(bf16[4,1024,256]{2,1,0:T(8,128)(2,1)} %bitcast.68), calls=%async_computation.3 | async-start | bytes 4194304 | tf_op jit(solution)/shard_map/all_to_all | solution.py:42
  142.2 2.0 gather_fusion
  144.3 3.2 pad_maximum_fusion.1
  147.4 28.3 %all-to-all-done.3 = bf16[4,1024,256]{2,1,0:T(8,128)(2,1)} async-done(((bf16[4,1024,256]{2,1,0:T(8,128)(2,1)}), bf16[4,1024,256]{2,1,0:T(8,128)(2,1)}, u32[]{:S(2)}, u32[]{:S(2)}) %all-to-all-start.3) | async-done | bytes 2097184 | tf_op jit(solution)/shard_map/all_to_all | solution.py:42
  175.7 4.5 %all-to-all-start.1 = ((bf16[4,1152,256]{2,1,0:T(8,128)(2,1)}), bf16[4,1152,256]{2,1,0:T(8,128)(2,1)}, u32[]{:S(2)}, u32[]{:S(2)}) async-start(bf16[4,1152,256]{2,1,0:T(8,128)(2,1)} %pad_maximum_fusion.1), calls=%async_computation.1 | async-start | bytes 4718592 | tf_op jit(solution)/shard_map/all_to_all | solution.py:42
  181.2 3.1 fusion.25
  184.4 23.9 %all-to-all-done.1 = bf16[4,1152,256]{2,1,0:T(8,128)(2,1)} async-done(((bf16[4,1152,256]{2,1,0:T(8,128)(2,1)}), bf16[4,1152,256]{2,1,0:T(8,128)(2,1)}, u32[]{:S(2)}, u32[]{:S(2)}) %all-to-all-start.1) | async-done | bytes 2359328 | tf_op jit(solution)/shard_map/all_to_all | solution.py:42
  208.3 3.4 select_reduce_fusion.2
  213.0 9.1 %all-gather.1 = f32[4,3,512]{2,1,0:T(4,128)S(1)} all-gather(f32[1,3,512]{2,1,0:T(4,128)S(1)} %maximum_bitcast_fusion), channel_id=2, replica_groups=mesh['dp'=64,'mp'=4] {'mp'}, dimensions={0}, use_global_device_ids=true | all-gather | bytes 30720 | tf_op jit(solution)/shard_map/all_gather | solution.py:61
  222.8 2.8 multiply_convert_fusion
  225.6 4.0 copy.33
  229.6 4.6 %all-to-all-start.6 = ((bf16[4,1024,256]{2,1,0:T(8,128)(2,1)}), bf16[4,1024,256]{2,1,0:T(8,128)(2,1)}, u32[]{:S(2)}, u32[]{:S(2)}) async-start(bf16[4,1024,256]{2,1,0:T(8,128)(2,1)} %bitcast.26), calls=%async_computation.7 | async-start | bytes 4194304 | tf_op jit(solution)/shard_map/all_to_all | solution.py:97
  234.2 2.1 exponential_select_fusion
  239.6 1.9 slice.86
  242.3 2.8 copy.32
  246.6 1.7 pad_maximum_fusion
  248.3 7.3 %all-to-all-done.6 = bf16[4,1024,256]{2,1,0:T(8,128)(2,1)} async-done(((bf16[4,1024,256]{2,1,0:T(8,128)(2,1)}), bf16[4,1024,256]{2,1,0:T(8,128)(2,1)}, u32[]{:S(2)}, u32[]{:S(2)}) %all-to-all-start.6) | async-done | bytes 2097184 | tf_op jit(solution)/shard_map/all_to_all | solution.py:97
  255.6 30.6 %all_to_all.42 = bf16[4,1280,256]{2,1,0:T(8,128)(2,1)} all-to-all(bf16[4,1280,256]{2,1,0:T(8,128)(2,1)} %pad_maximum_fusion), channel_id=1, replica_groups=mesh['dp'=64,'mp'=4] {'mp'}, dimensions={0} | all-to-all | bytes 5242880 | tf_op jit(solution)/shard_map/all_to_all | solution.py:97
  286.2 14.0 %all-to-all-start.7 = ((bf16[64,64,256]{2,1,0:T(8,128)(2,1)}), bf16[64,64,256]{2,1,0:T(8,128)(2,1)S(1)}, u32[]{:S(2)}, u32[]{:S(2)}) async-start(bf16[64,64,256]{2,1,0:T(8,128)(2,1)} %bitcast.27), calls=%async_computation.8 | async-start | bytes 4194304 | tf_op jit(solution)/shard_map/all_to_all | solution.py:106
  300.2 5.1 %fusion.7 = f32[512,4,256]{2,0,1:T(8,128)} fusion(bf16[4,1024,256]{2,1,0:T(8,128)(2,1)} %all-to-all-done.3, f32[1024,512]{1,0:T(8,128)} %copy-done.5, f32[512]{0:T(512)S(1)} %get-tuple-element.8, pred[1024]{0:T(1024)(128)(4,1)S(1)} %reshape.118), kind=kOutput, calls=%fused_computation.26 | convolution fusion | flops 1075314688 | bytes 6294528 | tf_op jit(solution)/shard_map/dot_general | solution.py:75
  306.7 44.7 %all-to-all-done.7 = bf16[64,64,256]{2,1,0:T(8,128)(2,1)S(1)} async-done(((bf16[64,64,256]{2,1,0:T(8,128)(2,1)}), bf16[64,64,256]{2,1,0:T(8,128)(2,1)S(1)}, u32[]{:S(2)}, u32[]{:S(2)}) %all-to-all-start.7) | async-done | bytes 2097184 | tf_op jit(solution)/shard_map/all_to_all | solution.py:106
  351.4 6.0 %all-to-all-start.5 = ((bf16[64,64,256]{2,1,0:T(8,128)(2,1)}), bf16[64,64,256]{2,1,0:T(8,128)(2,1)}, u32[]{:S(2)}, u32[]{:S(2)}) async-start(bf16[64,64,256]{2,1,0:T(8,128)(2,1)} %bitcast.67), calls=%async_computation.6 | async-start | bytes 4194304 | tf_op jit(solution)/shard_map/all_to_all | solution.py:106
  357.7 5.2 %add_multiply_fusion = f32[512,4,256]{2,0,1:T(8,128)} fusion(f32[512,4,256]{2,0,1:T(8,128)} %fusion.7, bf16[4,1152,256]{2,1,0:T(8,128)(2,1)} %all-to-all-done.1, bf16[1024,512]{1,0:T(8,128)(2,1)S(1)} %copy-done.8, bf16[128,512]{1,0:T(8,128)(2,1)S(1)} %fusion.10), kind=kOutput, calls=%fused_computation.20 | convolution fusion | flops 1211367424 | bytes 7733248 | tf_op jit(solution)/shard_map/dot_general | solution.py:75
  364.0 2.5 copy.35
  366.5 42.1 %all-to-all-done.5 = bf16[64,64,256]{2,1,0:T(8,128)(2,1)} async-done(((bf16[64,64,256]{2,1,0:T(8,128)(2,1)}), bf16[64,64,256]{2,1,0:T(8,128)(2,1)}, u32[]{:S(2)}, u32[]{:S(2)}) %all-to-all-start.5) | async-done | bytes 2097184 | tf_op jit(solution)/shard_map/all_to_all | solution.py:106
  408.6 2.8 copy.34
  412.1 4.4 %copy.36 = f32[32,128,256]{2,1,0:T(8,128)} copy(f32[32,128,256]{2,0,1:T(8,128)S(1)} %fusion) | data formatting | bytes 8388608 | tf_op jit(solution)/shard_map/kr,rpd->kpd/dot_general | solution.py:114
  416.6 7.3 %scatter_fusion = f32[4096,256]{1,0:T(8,128)} fusion(f32[4096,256]{1,0:T(8,128)} %bitcast.65, s32[512]{0:T(512)S(1)} %compare_select_fusion, f32[512,256]{1,0:T(8,128)S(1)} %bitcast.71), kind=kCustom, calls=%fused_computation.2 | custom fusion | flops 131072 | bytes 1574912 | tf_op jit(solution)/shard_map/scatter-add | solution.py:115
  (65 shorter events, 15.7 us)
Async XLA Ops:
  7.2 2.1 copy-start
  136.6 4.6 %copy-start.9 = (bf16[512,256]{1,0:T(8,128)(2,1)S(1)}, bf16[512,256]{1,0:T(8,128)(2,1)}, u32[]{:S(2)}) copy-start(bf16[512,256]{1,0:T(8,128)(2,1)} %param.4) | copy-start | bytes 786436
  136.6 5.5 %copy-start.10 = (s32[512]{0:T(512)S(1)}, s32[512]{0:T(512)}, u32[]{:S(2)}) copy-start(s32[512]{0:T(512)} %param.6) | copy-start | bytes 6148
  136.6 39.1 %all-to-all-start.3 = ((bf16[4,1024,256]{2,1,0:T(8,128)(2,1)}), bf16[4,1024,256]{2,1,0:T(8,128)(2,1)}, u32[]{:S(2)}, u32[]{:S(2)}) async-start(bf16[4,1024,256]{2,1,0:T(8,128)(2,1)} %bitcast.68), calls=%async_computation.3 | async-start | bytes 4194304 | tf_op jit(solution)/shard_map/all_to_all | solution.py:42
  141.2 40.0 %all-gather.4.cloned.1.call-start = ((), (), s32[]{:S(2)}) async-start(), calls=%async_computation.9 | async-start | bytes 1310720 | tf_op jit(solution)/shard_map/all_gather | solution.py:27
  175.7 32.5 %all-to-all-start.1 = ((bf16[4,1152,256]{2,1,0:T(8,128)(2,1)}), bf16[4,1152,256]{2,1,0:T(8,128)(2,1)}, u32[]{:S(2)}, u32[]{:S(2)}) async-start(bf16[4,1152,256]{2,1,0:T(8,128)(2,1)} %pad_maximum_fusion.1), calls=%async_computation.1 | async-start | bytes 4718592 | tf_op jit(solution)/shard_map/all_to_all | solution.py:42
  184.4 38.5 %copy-start.5 = (f32[1024,512]{1,0:T(8,128)}, f32[1024,512]{1,0:T(8,128)S(1)}, u32[]{:S(2)}) copy-start(f32[1024,512]{1,0:T(8,128)S(1)} %get-tuple-element.20) | copy-start | bytes 6291460
  211.6 1.4 copy-start.2
  211.7 11.1 %copy-start.11 = (bf16[512,1024]{0,1:T(8,128)(2,1)S(1)}, bf16[512,1024]{0,1:T(8,128)(2,1)}, u32[]{:S(2)}) copy-start(bf16[512,1024]{0,1:T(8,128)(2,1)} %all-gather.4.cloned.1.call-done) | copy-start | bytes 3145732
  229.6 26.0 %all-to-all-start.6 = ((bf16[4,1024,256]{2,1,0:T(8,128)(2,1)}), bf16[4,1024,256]{2,1,0:T(8,128)(2,1)}, u32[]{:S(2)}, u32[]{:S(2)}) async-start(bf16[4,1024,256]{2,1,0:T(8,128)(2,1)} %bitcast.26), calls=%async_computation.7 | async-start | bytes 4194304 | tf_op jit(solution)/shard_map/all_to_all | solution.py:97
  236.4 1.6 copy-start.12
  236.5 1.0 copy-start.7
  239.5 2.8 copy-start.6
  286.2 65.3 %all-to-all-start.7 = ((bf16[64,64,256]{2,1,0:T(8,128)(2,1)}), bf16[64,64,256]{2,1,0:T(8,128)(2,1)S(1)}, u32[]{:S(2)}, u32[]{:S(2)}) async-start(bf16[64,64,256]{2,1,0:T(8,128)(2,1)} %bitcast.27), calls=%async_computation.8 | async-start | bytes 4194304 | tf_op jit(solution)/shard_map/all_to_all | solution.py:106
  300.2 5.1 %copy-start.3 = (bf16[4,1280,256]{2,1,0:T(8,128)(2,1)S(1)}, bf16[4,1280,256]{2,1,0:T(8,128)(2,1)}, u32[]{:S(2)}) copy-start(bf16[4,1280,256]{2,1,0:T(8,128)(2,1)} %all_to_all.42) | copy-start | bytes 7864324
  306.7 51.0 %copy-start.8 = (bf16[1024,512]{1,0:T(8,128)(2,1)S(1)}, bf16[1024,512]{1,0:T(8,128)(2,1)}, u32[]{:S(2)}) copy-start(bf16[1024,512]{1,0:T(8,128)(2,1)} %copy-done.7) | copy-start | bytes 3145732
  351.4 57.2 %all-to-all-start.5 = ((bf16[64,64,256]{2,1,0:T(8,128)(2,1)}), bf16[64,64,256]{2,1,0:T(8,128)(2,1)}, u32[]{:S(2)}, u32[]{:S(2)}) async-start(bf16[64,64,256]{2,1,0:T(8,128)(2,1)} %bitcast.67), calls=%async_computation.6 | async-start | bytes 4194304 | tf_op jit(solution)/shard_map/all_to_all | solution.py:106
  357.5 66.5 %reduce-scatter.2.cloned.1.call-start = ((), (), s32[]{:S(2)}) async-start(), calls=%async_computation.10 | async-start | bytes 2621440 | tf_op jit(solution)/shard_map/reduce_scatter | solution.py:79
  366.5 44.9 %copy-start.4 = (bf16[64,64,256]{2,0,1:T(8,128)(2,1)S(1)}, bf16[64,64,256]{2,0,1:T(8,128)(2,1)}, u32[]{:S(2)}) copy-start(bf16[64,64,256]{2,0,1:T(8,128)(2,1)} %copy.35) | copy-start | bytes 6291460
  416.6 7.3 %copy-start.1 = (bf16[4096,256]{1,0:T(8,128)(2,1)S(1)}, bf16[4096,256]{1,0:T(8,128)(2,1)}, u32[]{:S(2)}) copy-start(bf16[4096,256]{1,0:T(8,128)(2,1)} %param.5) | copy-start | bytes 6291460
Sparse Core Ops, SparseCore 0:
  144.4 30.5 all-gather.3
  363.0 31.3 reduce-scatter.1
where the time goes:
time: 432 us; the launch traced here: 431 us
  blocking collectives  161 us (37%)
  waiting for transfers between devices  146 us (34%)
  starting transfers between devices  34 us (8%)
  local copies, waits for them, and re-layouts  29.2 us (7%)
  other arithmetic  24 us (6%)
  matrix products  21.8 us (5%)
  between operations  14.4 us (3%)
    all_to_all x2, blocking collectives, body(): lax.all_to_all(outgoing[:, h * part:(h + 1) * part], 'dp', split_axis=0,...  121 us
    all_to_all x2, waiting for transfers between devices, body(): lax.all_to_all(sent.reshape(dp_count, part, shard_width), 'dp', split_axi...  86.8 us
    all_to_all x2, waiting for transfers between devices, body(): lax.all_to_all(send, 'mp', split_axis=0, concat_axis=0, tiled=True)  52.2 us
    all_to_all x1, blocking collectives, body(): lax.all_to_all(jnp.concatenate(pieces, axis=1), 'mp', split_axis=0, conca...  30.6 us
    all_to_all x2, starting transfers between devices, body(): lax.all_to_all(sent.reshape(dp_count, part, shard_width), 'dp', split_axi...  20 us
    dot_general x2, matrix products, body(): lax.dot_general(g, c, (((0,), (1,)), ((), ())), preferred_element_type=jn...  10.2 us
    all_gather x1, blocking collectives, body(): lax.all_gather(jnp.stack([local_top, local_total, local_own]), 'mp', axis=0)  9.14 us
    all_to_all x2, starting transfers between devices, body(): lax.all_to_all(send, 'mp', split_axis=0, concat_axis=0, tiled=True)  9.09 us
  transfers between devices with their start and end apart: 7, of which 5 were waited for; matrix products, arithmetic and copies ran while one was open for 12% of the time, Pallas kernels for 0%

commit v1 on v0

--- a/solution.py
+++ b/solution.py
@@ -5,6 +5,29 @@
 
 PBS = 128
 HALVES = 2
+
+
+def cut_along(value, dim, size):
+    shape = value.shape
+    tiles = value.reshape(*shape[:dim], size, shape[dim] // size, *shape[dim + 1 :])
+    return jnp.moveaxis(tiles, dim, 0)
+
+
+def joined_along(pieces, dim):
+    pieces = jnp.moveaxis(pieces, 0, dim)
+    shape = pieces.shape
+    return pieces.reshape(*shape[:dim], shape[dim] * shape[dim + 1], *shape[dim + 2 :])
+
+
+def pairwise_exchange(value, axis, split_dim, concat_dim):
+    size, index = (lax.axis_size(axis), lax.axis_index(axis))
+    blocks = cut_along(value, split_dim, size)
+    outs = [blocks[index]]
+    for step in range(1, size):
+        sent = blocks[index ^ step]
+        outs.append(lax.ppermute(sent, axis, [(i, i ^ step) for i in range(size)]))
+    blocks = jnp.stack(outs)[index ^ jnp.arange(size)]
+    return joined_along(blocks, concat_dim)
 
 
 def body(queries, passages, positives, negatives):
@@ -39,7 +62,7 @@
                 [positive_rows.reshape(mp_count, pos_per, shard_width), send], axis=1
             )
             ok = jnp.concatenate([jnp.ones((pos_per,), bool), ok])
-        mine.append(lax.all_to_all(send, "mp", split_axis=0, concat_axis=0, tiled=True))
+        mine.append(pairwise_exchange(send, "mp", 0, 0))
         valid.append(ok)
     scores = [
         factor

time: 432 us -> 402 us (0.931)
  blocking collectives: 161 us -> 105 us
  local copies, waits for them, and re-layouts: 29.2 us -> 39 us
  waiting for transfers between devices: 146 us -> 155 us
    all_to_all x2 -> x1, blocking collectives: 121 us -> 64.3 us  [body(): lax.all_to_all(outgoing[:, h * part:(h + 1) * part], 'dp', split_axis=0,...]
    ppermute x0 -> x6, waiting for transfers between devices: none -> 18 us  [pairwise_exchange(): outs.append(lax.ppermute(sent, axis, [(i, i ^ step) for i in range(size)]))]
    all_to_all x2 -> x1, waiting for transfers between devices: 52.2 us -> 42.3 us  [body(): lax.all_to_all(outgoing[:, h * part:(h + 1) * part], 'dp', split_axis=0,...]
    ppermute x0 -> x6, starting transfers between devices: none -> 6.51 us  [pairwise_exchange(): outs.append(lax.ppermute(sent, axis, [(i, i ^ step) for i in range(size)]))]
    gather x0 -> x2, local copies, waits for them, and re-layouts: none -> 5.96 us  [pairwise_exchange(): blocks = jnp.stack(outs)[index ^ jnp.arange(size)]]
    another operation x1 -> x3, other arithmetic: 0.1 us -> 4.84 us  [the longest x2 4.74 us: pairwise_exchange(): blocks = jnp.stack(outs)[index ^ jnp.arange(size)]]
    all_to_all x2 -> x1, starting transfers between devices: 9.09 us -> 6.14 us  [body(): lax.all_to_all(outgoing[:, h * part:(h + 1) * part], 'dp', split_axis=0,...]
  transfers between devices with their start and end apart: 7 -> 12, of which waited for: 5 -> 6; matrix products, arithmetic and copies ran while one was open for 12% -> 15% of each run, Pallas kernels for 0% -> 0%
where the time goes in v1:
time: 402 us; the launch traced here: 400 us
  waiting for transfers between devices  155 us (39%)
  blocking collectives  105 us (26%)
  local copies, waits for them, and re-layouts  39 us (10%)
  starting transfers between devices  37.1 us (9%)
  other arithmetic  28.3 us (7%)
  matrix products  21.5 us (5%)
  between operations  14.4 us (4%)
    all_to_all x2, waiting for transfers between devices, body(): lax.all_to_all(sent.reshape(dp_count, part, shard_width), 'dp', split_axi...  86.8 us
    all_to_all x1, blocking collectives, body(): lax.all_to_all(outgoing[:, h * part:(h + 1) * part], 'dp', split_axis=0,...  64.3 us
    all_to_all x1, waiting for transfers between devices, body(): lax.all_to_all(outgoing[:, h * part:(h + 1) * part], 'dp', split_axis=0,...  42.3 us
    all_to_all x1, blocking collectives, body(): lax.all_to_all(jnp.concatenate(pieces, axis=1), 'mp', split_axis=0, conca...  31.2 us
    all_to_all x2, starting transfers between devices, body(): lax.all_to_all(sent.reshape(dp_count, part, shard_width), 'dp', split_axi...  19.8 us
    ppermute x6, waiting for transfers between devices, pairwise_exchange(): outs.append(lax.ppermute(sent, axis, [(i, i ^ step) for i in range(size)]))  18 us
    dot_general x2, matrix products, body(): lax.dot_general(g, c, (((0,), (1,)), ((), ())), preferred_element_type=jn...  10.2 us
    all_gather x1, blocking collectives, body(): lax.all_gather(jnp.stack([local_top, local_total, local_own]), 'mp', axis=0)  9.56 us
  transfers between devices with their start and end apart: 12, of which 6 were waited for; matrix products, arithmetic and copies ran while one was open for 15% of the time, Pallas kernels for 0%

profile of v1, /device:TPU:1, one launch (start us, length us, event | category | flops | bytes accessed | tf_op | source)
XLA Modules:
  0.0 400.5 jit_solution(2275240063830343689)
XLA Ops:
  9.3 2.8 gather_fusion.1
  12.1 2.7 select_select_fusion
  16.6 64.3 %all_to_all.30 = bf16[64,64,256]{2,1,0:T(8,128)(2,1)} all-to-all(bf16[64,64,256]{2,1,0:T(8,128)(2,1)S(1)} %get-tuple-element.11), channel_id=1, replica_groups=mesh['dp'=64,'mp'=4] {'dp'}, dimensions={0} | all-to-all | bytes 4194304 | tf_op jit(solution)/shard_map/all_to_all | solution.py:55
  80.9 6.1 %all-to-all-start = ((bf16[64,64,256]{2,1,0:T(8,128)(2,1)}), bf16[64,64,256]{2,1,0:T(8,128)(2,1)}, u32[]{:S(2)}, u32[]{:S(2)}) async-start(bf16[64,64,256]{2,1,0:T(8,128)(2,1)} %get-tuple-element.12), calls=%async_computation | async-start | bytes 4194304 | tf_op jit(solution)/shard_map/all_to_all | solution.py:55
  90.2 2.5 constant_dynamic-slice_fusion
  92.7 2.5 collective-permute-start.5
  95.9 42.3 %all-to-all-done = bf16[64,64,256]{2,1,0:T(8,128)(2,1)} async-done(((bf16[64,64,256]{2,1,0:T(8,128)(2,1)}), bf16[64,64,256]{2,1,0:T(8,128)(2,1)}, u32[]{:S(2)}, u32[]{:S(2)}) %all-to-all-start) | async-done | bytes 2097184 | tf_op jit(solution)/shard_map/all_to_all | solution.py:55
  138.2 2.8 fusion.11
  141.0 2.5 collective-permute-start.2
  148.9 3.1 fusion.31
  152.1 17.6 %collective-permute-done.2 = bf16[1,1152,256]{2,1,0:T(8,128)(2,1)} collective-permute-done((bf16[1,1152,256]{2,1,0:T(8,128)(2,1)}, bf16[1,1152,256]{2,1,0:T(8,128)(2,1)}, u32[]{:S(2)}, u32[]{:S(2)}) %collective-permute-start.2) | collective-permute-done | bytes 589856 | tf_op jit(solution)/shard_map/ppermute | solution.py:28
  170.0 3.1 maximum_bitcast_fusion
  173.1 3.9 gather_fusion.2
  177.0 3.1 select_reduce_fusion.2
  181.5 9.6 %all-gather.1 = f32[4,3,512]{2,1,0:T(4,128)S(1)} all-gather(f32[1,3,512]{2,1,0:T(4,128)S(1)} %maximum_bitcast_fusion.2), channel_id=2, replica_groups=mesh['dp'=64,'mp'=4] {'mp'}, dimensions={0}, use_global_device_ids=true | all-gather | bytes 30720 | tf_op jit(solution)/shard_map/all_gather | solution.py:84
  191.8 2.8 multiply_convert_fusion
  194.6 3.9 copy.33
  198.5 4.4 %all-to-all-start.4 = ((bf16[4,1024,256]{2,1,0:T(8,128)(2,1)}), bf16[4,1024,256]{2,1,0:T(8,128)(2,1)}, u32[]{:S(2)}, u32[]{:S(2)}) async-start(bf16[4,1024,256]{2,1,0:T(8,128)(2,1)} %bitcast.39), calls=%async_computation.5 | async-start | bytes 4194304 | tf_op jit(solution)/shard_map/all_to_all | solution.py:120
  203.0 2.1 exponential_select_fusion
  211.1 2.8 copy.32
  217.0 8.0 %all-to-all-done.4 = bf16[4,1024,256]{2,1,0:T(8,128)(2,1)} async-done(((bf16[4,1024,256]{2,1,0:T(8,128)(2,1)}), bf16[4,1024,256]{2,1,0:T(8,128)(2,1)}, u32[]{:S(2)}, u32[]{:S(2)}) %all-to-all-start.4) | async-done | bytes 2097184 | tf_op jit(solution)/shard_map/all_to_all | solution.py:120
  225.0 31.2 %all_to_all.31 = bf16[4,1280,256]{2,1,0:T(8,128)(2,1)} all-to-all(bf16[4,1280,256]{2,1,0:T(8,128)(2,1)} %pad_maximum_fusion), channel_id=1, replica_groups=mesh['dp'=64,'mp'=4] {'mp'}, dimensions={0} | all-to-all | bytes 5242880 | tf_op jit(solution)/shard_map/all_to_all | solution.py:120
  256.1 13.7 %all-to-all-start.5 = ((bf16[64,64,256]{2,1,0:T(8,128)(2,1)}), bf16[64,64,256]{2,1,0:T(8,128)(2,1)S(1)}, u32[]{:S(2)}, u32[]{:S(2)}) async-start(bf16[64,64,256]{2,1,0:T(8,128)(2,1)} %bitcast.40), calls=%async_computation.6 | async-start | bytes 4194304 | tf_op jit(solution)/shard_map/all_to_all | solution.py:129
  269.9 5.1 %fusion.7 = f32[512,4,256]{2,0,1:T(8,128)} fusion(bf16[4,1024,256]{2,1,0:T(8,128)(2,1)} %gather_fusion.3, f32[1024,512]{1,0:T(8,128)} %copy-done.5, f32[512]{0:T(512)S(1)} %get-tuple-element.8, pred[1024]{0:T(1024)(128)(4,1)S(1)} %reshape.145), kind=kOutput, calls=%fused_computation.37 | convolution fusion | flops 1075314688 | bytes 6294528 | tf_op jit(solution)/shard_map/dot_general | solution.py:98
  276.5 44.7 %all-to-all-done.5 = bf16[64,64,256]{2,1,0:T(8,128)(2,1)S(1)} async-done(((bf16[64,64,256]{2,1,0:T(8,128)(2,1)}), bf16[64,64,256]{2,1,0:T(8,128)(2,1)S(1)}, u32[]{:S(2)}, u32[]{:S(2)}) %all-to-all-start.5) | async-done | bytes 2097184 | tf_op jit(solution)/shard_map/all_to_all | solution.py:129
  321.1 6.0 %all-to-all-start.3 = ((bf16[64,64,256]{2,1,0:T(8,128)(2,1)}), bf16[64,64,256]{2,1,0:T(8,128)(2,1)}, u32[]{:S(2)}, u32[]{:S(2)}) async-start(bf16[64,64,256]{2,1,0:T(8,128)(2,1)} %bitcast.87), calls=%async_computation.4 | async-start | bytes 4194304 | tf_op jit(solution)/shard_map/all_to_all | solution.py:129
  327.4 5.2 %add_multiply_fusion = f32[512,4,256]{2,0,1:T(8,128)} fusion(f32[512,4,256]{2,0,1:T(8,128)} %fusion.7, bf16[4,1152,256]{2,1,0:T(8,128)(2,1)} %gather_fusion.2, bf16[1024,512]{1,0:T(8,128)(2,1)S(1)} %copy-done.8, bf16[128,512]{1,0:T(8,128)(2,1)S(1)} %fusion.15), kind=kOutput, calls=%fused_computation.27 | convolution fusion | flops 1211367424 | bytes 7733248 | tf_op jit(solution)/shard_map/dot_general | solution.py:98
  333.7 2.5 copy.35
  336.2 42.1 %all-to-all-done.3 = bf16[64,64,256]{2,1,0:T(8,128)(2,1)} async-done(((bf16[64,64,256]{2,1,0:T(8,128)(2,1)}), bf16[64,64,256]{2,1,0:T(8,128)(2,1)}, u32[]{:S(2)}, u32[]{:S(2)}) %all-to-all-start.3) | async-done | bytes 2097184 | tf_op jit(solution)/shard_map/all_to_all | solution.py:129
  378.3 2.8 copy.34
  381.8 4.4 %copy.36 = f32[32,128,256]{2,1,0:T(8,128)} copy(f32[32,128,256]{2,0,1:T(8,128)S(1)} %fusion) | data formatting | bytes 8388608 | tf_op jit(solution)/shard_map/kr,rpd->kpd/dot_general | solution.py:137
  386.3 7.3 %scatter_fusion = f32[4096,256]{1,0:T(8,128)} fusion(f32[4096,256]{1,0:T(8,128)} %bitcast.85, s32[512]{0:T(512)S(1)} %compare_select_fusion, f32[512,256]{1,0:T(8,128)S(1)} %bitcast.90), kind=kCustom, calls=%fused_computation.4 | custom fusion | flops 131072 | bytes 1574912 | tf_op jit(solution)/shard_map/scatter-add | solution.py:138
  (85 shorter events, 28.1 us)
Async XLA Ops:
  7.2 2.1 copy-start
  80.9 6.2 %copy-start.10 = (bf16[512,256]{1,0:T(8,128)(2,1)S(1)}, bf16[512,256]{1,0:T(8,128)(2,1)}, u32[]{:S(2)}) copy-start(bf16[512,256]{1,0:T(8,128)(2,1)} %param.4) | copy-start | bytes 786436
  80.9 7.1 %copy-start.11 = (s32[512]{0:T(512)S(1)}, s32[512]{0:T(512)}, u32[]{:S(2)}) copy-start(s32[512]{0:T(512)} %param.6) | copy-start | bytes 6148
  80.9 57.3 %all-to-all-start = ((bf16[64,64,256]{2,1,0:T(8,128)(2,1)}), bf16[64,64,256]{2,1,0:T(8,128)(2,1)}, u32[]{:S(2)}, u32[]{:S(2)}) async-start(bf16[64,64,256]{2,1,0:T(8,128)(2,1)} %get-tuple-element.12), calls=%async_computation | async-start | bytes 4194304 | tf_op jit(solution)/shard_map/all_to_all | solution.py:55
  87.1 61.8 %all-gather.4.cloned.1.call-start = ((), (), s32[]{:S(2)}) async-start(), calls=%async_computation.7 | async-start | bytes 1310720 | tf_op jit(solution)/shard_map/all_gather | solution.py:50
  92.7 51.3 %collective-permute-start.5 = (bf16[1,1024,256]{2,1,0:T(8,128)(2,1)}, bf16[1,1024,256]{2,1,0:T(8,128)(2,1)S(1)}, u32[]{:S(2)}, u32[]{:S(2)}) collective-permute-start(bf16[1,1024,256]{2,1,0:T(8,128)(2,1)} %get-tuple-element.18), channel_id=1, source_target_pairs={{0,3},{1,2},{2,1},{3,0},{4,7},{5,6},{6,5},{7,4},{8,11},{9,10},{10,... | collective-permute-start | bytes 1572872 | tf_op jit(solution)/shard_map/ppermute | solution.py:28
  95.2 50.0 %collective-permute-start.4 = (bf16[1,1024,256]{2,1,0:T(8,128)(2,1)S(1)}, bf16[1,1024,256]{2,1,0:T(8,128)(2,1)}, u32[]{:S(2)}, u32[]{:S(2)}) collective-permute-start(bf16[1,1024,256]{2,1,0:T(8,128)(2,1)S(1)} %get-tuple-element.19), channel_id=1, source_target_pairs={{0,2},{1,3},{2,0},{3,1},{4,6},{5,7},{6,4},{7,5},{8,10},{9,11},{10,... | collective-permute-start | bytes 1572872 | tf_op jit(solution)/shard_map/ppermute | solution.py:28
  95.7 49.5 %collective-permute-start.3 = (bf16[1,1024,256]{2,1,0:T(8,128)(2,1)S(1)}, bf16[1,1024,256]{2,1,0:T(8,128)(2,1)}, u32[]{:S(2)}, u32[]{:S(2)}) collective-permute-start(bf16[1,1024,256]{2,1,0:T(8,128)(2,1)S(1)} %get-tuple-element.20), channel_id=1, source_target_pairs={{0,1},{1,0},{2,3},{3,2},{4,5},{5,4},{6,7},{7,6},{8,9},{9,8},{10,11... | collective-permute-start | bytes 1572872 | tf_op jit(solution)/shard_map/ppermute | solution.py:28
  141.0 28.7 %collective-permute-start.2 = (bf16[1,1152,256]{2,1,0:T(8,128)(2,1)}, bf16[1,1152,256]{2,1,0:T(8,128)(2,1)}, u32[]{:S(2)}, u32[]{:S(2)}) collective-permute-start(bf16[1,1152,256]{2,1,0:T(8,128)(2,1)} %get-tuple-element.16), channel_id=1, source_target_pairs={{0,3},{1,2},{2,1},{3,0},{4,7},{5,6},{6,5},{7,4},{8,11},{9,10},{10,... | collective-permute-start | bytes 1769480 | tf_op jit(solution)/shard_map/ppermute | solution.py:28
  143.5 26.2 %collective-permute-start.1 = (bf16[1,1152,256]{2,1,0:T(8,128)(2,1)}, bf16[1,1152,256]{2,1,0:T(8,128)(2,1)}, u32[]{:S(2)}, u32[]{:S(2)}) collective-permute-start(bf16[1,1152,256]{2,1,0:T(8,128)(2,1)} %get-tuple-element.15), channel_id=1, source_target_pairs={{0,2},{1,3},{2,0},{3,1},{4,6},{5,7},{6,4},{7,5},{8,10},{9,11},{10,... | collective-permute-start | bytes 1769480 | tf_op jit(solution)/shard_map/ppermute | solution.py:28
  144.0 1.2 copy-start.9
  144.0 26.0 %collective-permute-start = (bf16[1,1152,256]{2,1,0:T(8,128)(2,1)}, bf16[1,1152,256]{2,1,0:T(8,128)(2,1)}, u32[]{:S(2)}, u32[]{:S(2)}) collective-permute-start(bf16[1,1152,256]{2,1,0:T(8,128)(2,1)} %get-tuple-element.14), channel_id=1, source_target_pairs={{0,1},{1,0},{2,3},{3,2},{4,5},{5,4},{6,7},{7,6},{8,9},{9,8},{10,11... | collective-permute-start | bytes 1769480 | tf_op jit(solution)/shard_map/ppermute | solution.py:28
  152.0 39.7 %copy-start.5 = (f32[1024,512]{1,0:T(8,128)}, f32[1024,512]{1,0:T(8,128)S(1)}, u32[]{:S(2)}) copy-start(f32[1024,512]{1,0:T(8,128)S(1)} %get-tuple-element.28) | copy-start | bytes 6291460
  173.1 3.9 copy-start.12
  180.1 1.4 copy-start.2
  180.2 11.5 %copy-start.13 = (bf16[512,1024]{0,1:T(8,128)(2,1)S(1)}, bf16[512,1024]{0,1:T(8,128)(2,1)}, u32[]{:S(2)}) copy-start(bf16[512,1024]{0,1:T(8,128)(2,1)} %all-gather.4.cloned.1.call-done) | copy-start | bytes 3145732
  198.5 26.5 %all-to-all-start.4 = ((bf16[4,1024,256]{2,1,0:T(8,128)(2,1)}), bf16[4,1024,256]{2,1,0:T(8,128)(2,1)}, u32[]{:S(2)}, u32[]{:S(2)}) async-start(bf16[4,1024,256]{2,1,0:T(8,128)(2,1)} %bitcast.39), calls=%async_computation.5 | async-start | bytes 4194304 | tf_op jit(solution)/shard_map/all_to_all | solution.py:120
  205.1 1.6 copy-start.14
  205.3 1.0 copy-start.7
  208.3 2.8 copy-start.6
  256.1 65.0 %all-to-all-start.5 = ((bf16[64,64,256]{2,1,0:T(8,128)(2,1)}), bf16[64,64,256]{2,1,0:T(8,128)(2,1)S(1)}, u32[]{:S(2)}, u32[]{:S(2)}) async-start(bf16[64,64,256]{2,1,0:T(8,128)(2,1)} %bitcast.40), calls=%async_computation.6 | async-start | bytes 4194304 | tf_op jit(solution)/shard_map/all_to_all | solution.py:129
  269.9 5.1 %copy-start.3 = (bf16[4,1280,256]{2,1,0:T(8,128)(2,1)S(1)}, bf16[4,1280,256]{2,1,0:T(8,128)(2,1)}, u32[]{:S(2)}) copy-start(bf16[4,1280,256]{2,1,0:T(8,128)(2,1)} %all_to_all.31) | copy-start | bytes 7864324
  276.4 51.0 %copy-start.8 = (bf16[1024,512]{1,0:T(8,128)(2,1)S(1)}, bf16[1024,512]{1,0:T(8,128)(2,1)}, u32[]{:S(2)}) copy-start(bf16[1024,512]{1,0:T(8,128)(2,1)} %copy-done.7) | copy-start | bytes 3145732
  321.1 57.2 %all-to-all-start.3 = ((bf16[64,64,256]{2,1,0:T(8,128)(2,1)}), bf16[64,64,256]{2,1,0:T(8,128)(2,1)}, u32[]{:S(2)}, u32[]{:S(2)}) async-start(bf16[64,64,256]{2,1,0:T(8,128)(2,1)} %bitcast.87), calls=%async_computation.4 | async-start | bytes 4194304 | tf_op jit(solution)/shard_map/all_to_all | solution.py:129
  327.2 66.4 %reduce-scatter.2.cloned.1.call-start = ((), (), s32[]{:S(2)}) async-start(), calls=%async_computation.8 | async-start | bytes 2621440 | tf_op jit(solution)/shard_map/reduce_scatter | solution.py:102
  336.2 44.9 %copy-start.4 = (bf16[64,64,256]{2,0,1:T(8,128)(2,1)S(1)}, bf16[64,64,256]{2,0,1:T(8,128)(2,1)}, u32[]{:S(2)}) copy-start(bf16[64,64,256]{2,0,1:T(8,128)(2,1)} %copy.35) | copy-start | bytes 6291460
  386.3 7.3 %copy-start.1 = (bf16[4096,256]{1,0:T(8,128)(2,1)S(1)}, bf16[4096,256]{1,0:T(8,128)(2,1)}, u32[]{:S(2)}) copy-start(bf16[4096,256]{1,0:T(8,128)(2,1)} %param.5) | copy-start | bytes 6291460
Sparse Core Ops, SparseCore 0:
  89.7 37.7 all-gather.3
  332.8 31.3 reduce-scatter.1
